TPU v7x, 256 devices: a whole 4x4x8 slice. The times are simulated.
256 devices in a mesh: dp: 32 (over x, z), tensor: 8 (over y, core).
Axes of the slice: x: 4, y: 4, z: 8, core: 2. Of those that a mesh axis runs over, the one named last changes fastest.
Arguments:
- counts: int32 [32], replicated, may hold values from 1 to 32, 512 in all
- keys: bfloat16 [1024, 28672], P('dp'), may hold values from -6 to 6
- inverse_cov: bfloat16 [28672, 28672], P('tensor', 'dp'), as said below
- hidden: bfloat16 [1024, 8192], P('dp', 'tensor'), may hold values from -6 to 6
- targets: bfloat16 [1024, 8192], P('dp', 'tensor'), may hold values from -48 to 48
- down_weight: bfloat16 [8192, 28672], P('tensor', 'dp'), may hold values from -0.03125 to 0.03125
Outputs:
- new_weight: bfloat16 [8192, 28672], P('tensor', 'dp')
- next_resid: bfloat16 [1024, 8192], P('dp', 'tensor')
Inputs may be any that keep to these rules, and one draw needn't show every extreme that they name: Group g has counts[g] live edits in its first counts[g] slots; the counts sum to 512; some group holds 32. `inverse_cov`: symmetric positive definite.
All inputs are finite; a program needn't handle non-finite values.
Results may differ from a plain program's by a relative error of at most 0.01.
The roundings to bfloat16 on the way count: a program that leaves them out, or rounds other values in their place, can miss the bound.
Values may be sent and summed in bfloat16 or wider, within the bound.
No kernel may reach another device: no remote copies, remote signals or barrier semaphores. Data moves between devices by JAX's collectives and lax.ppermute only.
A program may use at most 128 MiB of HBM per device.

v0:
```python
import jax
import jax.numpy as jnp
from jax import lax
from jax.sharding import PartitionSpec as P

LAYERS_LEFT = 3


def cholesky_solve(system, right_side):
    factor = jnp.linalg.cholesky(system)
    middle = lax.linalg.triangular_solve(factor, right_side, left_side=True, lower=True)
    return lax.linalg.triangular_solve(factor, middle, left_side=True, lower=True, transpose_a=True)


def rows_product(left, right):
    return lax.dot_general(
        left, right, (((1,), (1,)), ((), ())), preferred_element_type=jnp.float32
    )


def pick(select, values):
    return jnp.dot(select, values, preferred_element_type=jnp.float32).astype(values.dtype)


def per_device(counts, keys, inverse_cov, hidden, targets, down_weight):
    slot_count = keys.shape[0]
    group_size = lax.axis_size("dp")
    group_index = lax.axis_index("dp")
    tensor_index = lax.axis_index("tensor")
    width_part = inverse_cov.shape[0]
    row_total = slot_count * group_size
    live_total = row_total // 2
    ends = jnp.cumsum(counts)
    starts = ends - counts
    compact = jnp.arange(live_total, dtype=jnp.int32)
    owner = jnp.minimum(jnp.sum(compact[:, None] >= ends[None, :], axis=1), group_size - 1)
    row_of = owner * slot_count + compact - starts[owner]
    select = (row_of[:, None] == jnp.arange(row_total, dtype=jnp.int32)[None, :]).astype(
        jnp.bfloat16
    )
    slots = jnp.arange(slot_count, dtype=jnp.int32)
    live_vec = slots < counts[group_index]
    live_slot = live_vec[:, None]
    own_compact = jnp.where(live_vec, starts[group_index] + slots, 0)
    masked_keys = jnp.where(live_slot, keys, jnp.zeros_like(keys))
    column_part = lax.dynamic_slice_in_dim(masked_keys, tensor_index * width_part, width_part, 1)
    columns = lax.all_to_all(masked_keys, "dp", split_axis=1, concat_axis=0, tiled=True)
    gathered = lax.all_gather(column_part, "dp", axis=0, tiled=True)
    keys_c = pick(select, gathered)
    columns_c = pick(select, columns)
    partial_q = jnp.dot(keys_c, inverse_cov, preferred_element_type=jnp.float32)
    precond_c = lax.psum(partial_q, "tensor").astype(jnp.bfloat16)
    gram_c = lax.psum(rows_product(precond_c, columns_c), "dp")
    base_partial = rows_product(columns, down_weight)
    gram_c, base_partial = lax.optimization_barrier((gram_c, base_partial))
    base = lax.psum_scatter(base_partial, "dp", scatter_dimension=0, tiled=True)
    system = gram_c + jnp.eye(live_total, dtype=jnp.float32)
    change = (targets.astype(jnp.float32) - hidden.astype(jnp.float32)) / LAYERS_LEFT
    resid_local = jnp.where(live_slot, change, jnp.zeros_like(change)).astype(jnp.bfloat16)
    resid_all = lax.all_gather(resid_local, "dp", axis=0, tiled=True)
    resid_c = pick(select, resid_all)
    solved_c = cholesky_solve(system, resid_c.astype(jnp.float32)).astype(jnp.bfloat16)
    weight_delta = lax.dot_general(
        solved_c, precond_c, (((0,), (0,)), ((), ())), preferred_element_type=jnp.float32
    )
    new_weight = (down_weight.astype(jnp.float32) + weight_delta).astype(jnp.bfloat16)
    gram_own = jnp.where(live_slot, jnp.take(gram_c, own_compact, axis=1).T, 0.0)
    extra = jnp.dot(
        gram_own,
        solved_c.astype(jnp.float32),
        precision=lax.Precision.HIGHEST,
        preferred_element_type=jnp.float32,
    )
    summed = hidden.astype(jnp.float32) + (base + extra)
    next_resid = jnp.where(live_slot, summed, jnp.zeros_like(summed)).astype(jnp.bfloat16)
    return (new_weight, next_resid)


def solution(mesh):
    in_specs = (
        P(),
        P("dp", None),
        P("tensor", "dp"),
        P("dp", "tensor"),
        P("dp", "tensor"),
        P("tensor", "dp"),
    )
    out_specs = (P("tensor", "dp"), P("dp", "tensor"))
    return jax.shard_map(
        per_device, mesh=mesh, in_specs=in_specs, out_specs=out_specs, check_vma=False
    )
```

profile of v0, /device:TPU:8, one launch (start us, length us, event | category | flops | bytes accessed | tf_op | source)
XLA Modules:
  0.0 581.5 jit_solution(14730715012602335396)
XLA Ops:
  7.2 1.2 dynamic_slice.9
  9.0 1.7 broadcast_select_fusion
  10.7 0.7 constant_dynamic-slice_fusion.1
  11.4 1.4 copy.29
  12.8 11.4 %all-to-all-start = ((bf16[32,32,896]{2,0,1:T(8,128)(2,1)}), bf16[32,32,896]{2,0,1:T(8,128)(2,1)S(1)}, u32[]{:S(2)}, u32[]{:S(2)}) async-start(bf16[32,32,896]{2,0,1:T(8,128)(2,1)} %bitcast.118), calls=%async_computation | async-start | bytes 3670016 | tf_op jit(solution)/shard_map/all_to_all | solution.py:47
  24.3 0.7 fusion.49
  25.5 0.7 fusion.84
  26.2 0.7 fusion.83
  26.9 4.5 compare_select_fusion.1
  31.6 15.7 %select_subtract_fusion = s32[512]{0:T(512)S(1)} fusion(pred[512]{0:T(512)(128)(4,1)S(1)} %get-tuple-element.38, pred[512]{0:T(512)(128)(4,1)S(1)} %get-tuple-element.37, pred[512]{0:T(512)(128)(4,1)S(1)} %get-tuple-element.36, pred[512]{0:T(512)(128)(4,1)S(1)} %get-tuple-element.35, pred[512]{0:T(512)(128)(4,1)S(1)} %get-tuple-element.34, ...), kind=kLoop, calls=%fused_computation.145 | loop fusion | flops 14848 | bytes 19044 | tf_op jit(solution)/shard_map/sub | solution.py:37
  47.8 1.2 fusion.73
  49.0 69.0 %all-gather.3.cloned.1.call-done = bf16[1024,3584]{1,0:T(8,128)(2,1)} async-done(((bf16[32,3584]{1,0:T(8,128)(2,1)}), bf16[1024,3584]{1,0:T(8,128)(2,1)}) %all-gather.3.cloned.1.call-update) | async-done | bytes 7340048 | tf_op jit(solution)/shard_map/all_gather | solution.py:48
  118.0 14.0 %fusion.35 = f32[512,896]{1,0:T(8,128)} fusion(bf16[3584,896]{1,0:T(8,128)(2,1)} %param.8, bf16[1024,3584]{1,0:T(8,128)(2,1)} %all-gather.3.cloned.1.call-done, s32[512]{0:T(512)S(1)} %select_subtract_fusion), kind=kOutput, calls=%fused_computation.56 | convolution fusion | flops 7048790016 | bytes 15599616 | tf_op jit(solution)/shard_map/dot_general | solution.py:51
  132.0 50.5 %all-reduce.5 = bf16[512,896]{1,0:T(8,128)(2,1)S(1)} all-reduce(f32[512,896]{1,0:T(8,128)} %fusion.35), channel_id=1, replica_groups=mesh['dp'=32,'tensor'=8] {'tensor'}, use_global_device_ids=true, to_apply=%region_2.3 | all-reduce | flops 458752 | bytes 2752512 | tf_op jit(solution)/shard_map/psum | solution.py:52
  182.5 2.8 fusion.36
  185.6 1.7 compare_and_fusion
  187.4 5.8 fusion.89
  193.2 3.1 all-gather.5.cloned.1.call-done
  196.3 4.5 fusion.85
  200.8 146.6 %all-reduce.4.cloned.1.call-done = f32[512,512]{0,1:T(8,128)} async-done(((f32[512,512]{0,1:T(8,128)}), f32[512,512]{0,1:T(8,128)}) %all-reduce.4.cloned.1.call-update) | async-done | bytes 1048592 | tf_op jit(solution)/shard_map/psum | solution.py:53
  347.4 1.3 convert_add_fusion
  349.1 1.2 copy-done
  350.6 11.7 %cholesky.104 = f32[128,128]{1,0:T(8,128)S(1)} custom-call(f32[128,128]{1,0:T(8,128)S(1)} %cholesky.266), custom_call_target="Cholesky" | custom-call | tf_op jit(solution)/shard_map/jit(cholesky)/cholesky | solution.py:10
  362.4 9.8 %custom-call.32 = f32[1,128,128]{1,2,0:T(8,128)S(1)} custom-call(f32[1,128,128]{2,1,0:T(8,128)S(1)} %get-tuple-element.60), custom_call_target="InvertDiagBlocksLowerTriangular" | custom-call | tf_op jit(solution)/shard_map/jit(cholesky)/cholesky | solution.py:10
  372.9 12.1 %cholesky.217 = f32[128,128]{1,0:T(8,128)S(1)} custom-call(f32[128,128]{1,0:T(8,128)S(1)} %cholesky.270), custom_call_target="Cholesky" | custom-call | tf_op jit(solution)/shard_map/jit(cholesky)/cholesky | solution.py:10
  385.1 9.8 %custom-call.33 = f32[1,128,128]{1,2,0:T(8,128)S(1)} custom-call(f32[1,128,128]{2,1,0:T(8,128)S(1)} %get-tuple-element.57), custom_call_target="InvertDiagBlocksLowerTriangular" | custom-call | tf_op jit(solution)/shard_map/jit(cholesky)/cholesky | solution.py:10
  395.5 11.7 %cholesky.238 = f32[128,128]{1,0:T(8,128)S(1)} custom-call(f32[128,128]{1,0:T(8,128)S(1)} %cholesky.275), custom_call_target="Cholesky" | custom-call | tf_op jit(solution)/shard_map/jit(cholesky)/cholesky | solution.py:10
  407.3 9.8 %custom-call.34 = f32[1,128,128]{1,2,0:T(8,128)S(1)} custom-call(f32[1,128,128]{2,1,0:T(8,128)S(1)} %get-tuple-element.54), custom_call_target="InvertDiagBlocksLowerTriangular" | custom-call | tf_op jit(solution)/shard_map/jit(cholesky)/cholesky | solution.py:10
  417.7 11.9 %cholesky.255 = f32[128,128]{1,0:T(8,128)S(1)} custom-call(f32[128,128]{1,0:T(8,128)S(1)} %convolution_subtract_fusion.6), custom_call_target="Cholesky" | custom-call | tf_op jit(solution)/shard_map/jit(cholesky)/cholesky | solution.py:10
  429.6 0.6 compare_reduce_fusion.27
  431.4 0.6 compare_reduce_fusion.26
  432.7 0.6 compare_reduce_fusion.25
  434.7 10.0 %while.1 = (s32[]{:T(128)}, f32[512,512]{1,0:T(8,128)S(1)}, s32[4,2]{0,1:T(2,128)S(1)}, f32[4,128,128]{2,1,0:T(8,128)}, s32[]{:T(128)}) while((s32[]{:T(128)}, f32[512,512]{1,0:T(8,128)S(1)}, s32[4,2]{0,1:T(2,128)S(1)}, f32[4,128,128]{2,1,0:T(8,128)}, s32[]{:T(128)}) %tuple.93), condition=%wide.while_cond, body=%wide.while_body.sunk | while | flops 2 | bytes 132205 | solution.py:12
  435.3 1.9 bitcast_dynamic-update-slice_fusion.2
  437.8 1.9 bitcast_dynamic-update-slice_fusion.2
  440.3 1.9 bitcast_dynamic-update-slice_fusion.2
  442.8 1.9 bitcast_dynamic-update-slice_fusion.2
  444.7 40.1 %custom-call.35 = f32[4,128,128]{1,2,0:T(8,128)S(1)} custom-call(f32[4,128,128]{2,1,0:T(8,128)} %get-tuple-element.13), custom_call_target="InvertDiagBlocksLowerTriangular" | custom-call | tf_op jit(solution)/shard_map/triangular_solve | solution.py:12
  485.5 1.5 fusion.39
  487.0 1.6 convolution_subtract_fusion.3
  488.6 0.6 fusion.64
  489.3 0.7 convolution_subtract_fusion.1
  490.6 1.1 fusion.19
  494.2 0.7 convolution_subtract_fusion
  495.6 1.1 fusion.16
  497.3 2.6 add_convert_fusion
  499.9 72.7 %reduce-scatter.2.cloned.1.call-done = f32[32,1024]{1,0:T(8,128)} async-done(((f32[1024,1024]{1,0:T(8,128)}), f32[32,1024]{1,0:T(8,128)}) %reduce-scatter.2.cloned.1.call-update) | async-done | bytes 131088 | tf_op jit(solution)/shard_map/reduce_scatter | solution.py:56
  572.6 2.2 fusion.24
  (71 shorter events, 12.6 us)
Async XLA Ops:
  7.2 110.9 %all-gather.3.cloned.1.call-start = ((), (), s32[]{:S(2)}) async-start(), calls=%async_computation.2 | async-start | bytes 7569408 | tf_op jit(solution)/shard_map/all_gather | solution.py:48
  12.8 11.5 %copy-start.4 = (bf16[32,1024]{1,0:T(8,128)(2,1)S(1)}, bf16[32,1024]{1,0:T(8,128)(2,1)}, u32[]{:S(2)}) copy-start(bf16[32,1024]{1,0:T(8,128)(2,1)} %param.10) | copy-start | bytes 196612
  12.8 11.5 %copy-start.5 = (bf16[32,1024]{1,0:T(8,128)(2,1)S(1)}, bf16[32,1024]{1,0:T(8,128)(2,1)}, u32[]{:S(2)}) copy-start(bf16[32,1024]{1,0:T(8,128)(2,1)} %param.9) | copy-start | bytes 196612
  12.8 12.3 %copy-start.6 = (s32[32]{0:T(128)S(1)}, s32[32]{0:T(128)}, u32[]{:S(2)}) copy-start(s32[32]{0:T(128)} %param.6) | copy-start | bytes 388
  12.8 169.7 %all-to-all-start = ((bf16[32,32,896]{2,0,1:T(8,128)(2,1)}), bf16[32,32,896]{2,0,1:T(8,128)(2,1)S(1)}, u32[]{:S(2)}, u32[]{:S(2)}) async-start(bf16[32,32,896]{2,0,1:T(8,128)(2,1)} %bitcast.118), calls=%async_computation | async-start | bytes 3670016 | tf_op jit(solution)/shard_map/all_to_all | solution.py:47
  24.3 172.0 %all-gather.5.cloned.1.call-start = ((), (), s32[]{:S(2)}) async-start(), calls=%async_computation.4 | async-start | bytes 2162688 | tf_op jit(solution)/shard_map/all_gather | solution.py:60
  25.1 322.4 %all-reduce.4.cloned.1.call-start = ((), (), s32[]{:S(2)}) async-start(), calls=%async_computation.3 | async-start | bytes 2097152 | tf_op jit(solution)/shard_map/psum | solution.py:53
  182.5 2.8 copy-start.2
  185.4 387.2 %reduce-scatter.2.cloned.1.call-start = ((), (), s32[]{:S(2)}) async-start(), calls=%async_computation.5 | async-start | bytes 4325376 | tf_op jit(solution)/shard_map/reduce_scatter | solution.py:56
  349.1 1.2 copy-start
  485.5 3.8 copy-start.1
  495.5 1.7 copy-start.3
  495.5 1.8 copy-start.7
  497.3 75.2 %copy-start.8 = (pred[32]{0:T(512)(128)(4,1)S(1)}, pred[32]{0:T(512)(128)(4,1)}, u32[]{:S(2)}) copy-start(pred[32]{0:T(512)(128)(4,1)} %compare_and_fusion) | copy-start | bytes 100
Sparse Core Ops, SparseCore 0:
  11.5 106.4 all-gather.2
  121.2 75.0 all-gather.4
  199.7 147.6 all-reduce.3
  351.2 221.3 reduce-scatter.1
where the time goes:
time: 589 us; the launch traced here: 582 us
  waiting for transfers between devices  291 us (49%)
  other arithmetic  148 us (25%)
  blocking collectives  50.5 us (9%)
  matrix products  45.4 us (8%)
  local copies, waits for them, and re-layouts  17.8 us (3%)
  between operations  16.9 us (3%)
  starting transfers between devices  11.8 us (2%)
    psum x1, waiting for transfers between devices, per_device(): gram_c = lax.psum(rows_product(precond_c, columns_c), 'dp')  147 us
    another operation x14, other arithmetic, cholesky_solve(): factor = jnp.linalg.cholesky(system)  78.9 us
    reduce_scatter x1, waiting for transfers between devices, per_device(): base = lax.psum_scatter(base_partial, 'dp', scatter_dimension=0, tiled=True)  72.7 us
    all_gather x1, waiting for transfers between devices, per_device(): gathered = lax.all_gather(column_part, 'dp', axis=0, tiled=True)  69 us
    psum x1, blocking collectives, per_device(): precond_c = lax.psum(partial_q, 'tensor').astype(jnp.bfloat16)  50.5 us
    another operation x3, other arithmetic, cholesky_solve(): lax.linalg.triangular_solve(factor, middle, left_side=True, lower=True, t...  40.7 us
    sub x1, other arithmetic, per_device(): row_of = owner * slot_count + compact - starts[owner]  15.7 us
    dot_general x1, matrix products, per_device(): partial_q = jnp.dot(keys_c, inverse_cov, preferred_element_type=jnp.float32)  14 us
  transfers between devices with their start and end apart: 5, of which 4 were waited for; matrix products, arithmetic and copies ran while one was open for 35% of the time, Pallas kernels for 0%

commit v1 on v0

--- a/solution.py
+++ b/solution.py
@@ -50,7 +50,7 @@
     columns_c = pick(select, columns)
     partial_q = jnp.dot(keys_c, inverse_cov, preferred_element_type=jnp.float32)
     precond_c = lax.psum(partial_q, "tensor").astype(jnp.bfloat16)
-    gram_c = lax.psum(rows_product(precond_c, columns_c), "dp")
+    gram_c = jnp.sum(lax.all_gather(rows_product(precond_c, columns_c), "dp"), axis=0)
     base_partial = rows_product(columns, down_weight)
     gram_c, base_partial = lax.optimization_barrier((gram_c, base_partial))
     base = lax.psum_scatter(base_partial, "dp", scatter_dimension=0, tiled=True)

time: 589 us -> 681 us (1.16)
  waiting for transfers between devices: 291 us -> 372 us
  other arithmetic: 148 us -> 158 us
    all_gather x0 -> x1, waiting for transfers between devices: none -> 228 us  [per_device(): lax.all_gather(rows_product(precond_c, columns_c), 'dp')]
    psum x1 -> x0, waiting for transfers between devices: 147 us -> none  [per_device(): gram_c = lax.psum(rows_product(precond_c, columns_c), 'dp')]
    reduce_sum x0 -> x1, other arithmetic: none -> 12.4 us  [per_device(): jnp.sum(lax.all_gather(rows_product(precond_c, columns_c), 'dp'), axis=0)]
  transfers between devices with their start and end apart: 5 -> 5, of which waited for: 4 -> 4; matrix products, arithmetic and copies ran while one was open for 35% -> 30% of each run, Pallas kernels for 0% -> 0%
where the time goes in v1:
time: 681 us; the launch traced here: 672 us
  waiting for transfers between devices  372 us (55%)
  other arithmetic  158 us (23%)
  blocking collectives  50.5 us (7%)
  matrix products  45.5 us (7%)
  local copies, waits for them, and re-layouts  17.8 us (3%)
  between operations  17 us (2%)
  starting transfers between devices  11.6 us (2%)
    all_gather x1, waiting for transfers between devices, per_device(): lax.all_gather(rows_product(precond_c, columns_c), 'dp')  228 us
    another operation x14, other arithmetic, cholesky_solve(): factor = jnp.linalg.cholesky(system)  78.9 us
    all_gather x1, waiting for transfers between devices, per_device(): gathered = lax.all_gather(column_part, 'dp', axis=0, tiled=True)  71.1 us
    reduce_scatter x1, waiting for transfers between devices, per_device(): base = lax.psum_scatter(base_partial, 'dp', scatter_dimension=0, tiled=True)  70.8 us
    psum x1, blocking collectives, per_device(): precond_c = lax.psum(partial_q, 'tensor').astype(jnp.bfloat16)  50.5 us
    another operation x3, other arithmetic, cholesky_solve(): lax.linalg.triangular_solve(factor, middle, left_side=True, lower=True, t...  40.8 us
    sub x1, other arithmetic, per_device(): row_of = owner * slot_count + compact - starts[owner]  15.2 us
    dot_general x1, matrix products, per_device(): partial_q = jnp.dot(keys_c, inverse_cov, preferred_element_type=jnp.float32)  14 us
  transfers between devices with their start and end apart: 5, of which 4 were waited for; matrix products, arithmetic and copies ran while one was open for 30% of the time, Pallas kernels for 0%

profile of v1, /device:TPU:8, one launch (start us, length us, event | category | flops | bytes accessed | tf_op | source)
XLA Modules:
  0.0 672.3 jit_solution(10021037839605141730)
XLA Ops:
  7.2 1.3 dynamic_slice.9
  9.1 1.7 broadcast_select_fusion
  10.8 0.7 constant_dynamic-slice_fusion.1
  11.5 1.5 copy.27
  13.0 11.4 %all-to-all-start = ((bf16[32,32,896]{2,0,1:T(8,128)(2,1)}), bf16[32,32,896]{2,0,1:T(8,128)(2,1)S(1)}, u32[]{:S(2)}, u32[]{:S(2)}) async-start(bf16[32,32,896]{2,0,1:T(8,128)(2,1)} %bitcast.120), calls=%async_computation | async-start | bytes 3670016 | tf_op jit(solution)/shard_map/all_to_all | solution.py:47
  24.5 0.7 fusion.49
  25.7 0.7 fusion.84
  26.4 0.7 fusion.83
  27.1 4.2 compare_select_fusion.1
  31.5 15.2 %select_subtract_fusion = s32[512]{0:T(512)S(1)} fusion(pred[512]{0:T(512)(128)(4,1)S(1)} %get-tuple-element.38, pred[512]{0:T(512)(128)(4,1)S(1)} %get-tuple-element.37, pred[512]{0:T(512)(128)(4,1)S(1)} %get-tuple-element.36, pred[512]{0:T(512)(128)(4,1)S(1)} %get-tuple-element.35, pred[512]{0:T(512)(128)(4,1)S(1)} %get-tuple-element.34, ...), kind=kLoop, calls=%fused_computation.145 | loop fusion | flops 14848 | bytes 19044 | tf_op jit(solution)/shard_map/sub | solution.py:37
  46.7 71.1 %all-gather.5.cloned.1.call-done = bf16[1024,3584]{1,0:T(8,128)(2,1)} async-done(((bf16[32,3584]{1,0:T(8,128)(2,1)}), bf16[1024,3584]{1,0:T(8,128)(2,1)}) %all-gather.5.cloned.1.call-update) | async-done | bytes 7340048 | tf_op jit(solution)/shard_map/all_gather | solution.py:48
  117.8 14.0 %fusion.35 = f32[512,896]{1,0:T(8,128)} fusion(bf16[3584,896]{1,0:T(8,128)(2,1)} %param.8, bf16[1024,3584]{1,0:T(8,128)(2,1)} %all-gather.5.cloned.1.call-done, s32[512]{0:T(512)S(1)} %select_subtract_fusion), kind=kOutput, calls=%fused_computation.56 | convolution fusion | flops 7048790016 | bytes 15599616 | tf_op jit(solution)/shard_map/dot_general | solution.py:51
  131.8 50.5 %all-reduce.2 = bf16[512,896]{1,0:T(8,128)(2,1)S(1)} all-reduce(f32[512,896]{1,0:T(8,128)} %fusion.35), channel_id=1, replica_groups=mesh['dp'=32,'tensor'=8] {'tensor'}, use_global_device_ids=true, to_apply=%region_2.3 | all-reduce | flops 458752 | bytes 2752512 | tf_op jit(solution)/shard_map/psum | solution.py:52
  182.3 2.8 fusion.36
  185.8 1.2 fusion.73
  186.9 1.7 compare_and_fusion
  188.6 5.9 fusion.89
  194.5 1.5 all-gather.7.cloned.1.call-done
  196.1 4.5 fusion.85
  200.6 228.2 %all-gather.9.cloned.1.call-done = f32[16384,512]{1,0:T(8,128)} async-done(((f32[512,512]{1,0:T(8,128)}), f32[16384,512]{1,0:T(8,128)}) %all-gather.9.cloned.1.call-update) | async-done | bytes 33554448 | tf_op jit(solution)/shard_map/all_gather | solution.py:53
  428.8 12.4 %reduce_sum.19 = f32[512,512]{1,0:T(8,128)S(1)} reduce(f32[32,512,512]{2,1,0:T(8,128)} %bitcast.118, f32[]{:T(128)} %constant.183.clone.1), dimensions={0}, to_apply=%region_3.4 | reduce | flops 8126464 | bytes 34603012 | tf_op jit(solution)/shard_map/reduce_sum | solution.py:53
  442.3 11.7 %cholesky.104 = f32[128,128]{1,0:T(8,128)S(1)} custom-call(f32[128,128]{1,0:T(8,128)S(1)} %cholesky.266), custom_call_target="Cholesky" | custom-call | tf_op jit(solution)/shard_map/jit(cholesky)/cholesky | solution.py:10
  454.2 9.8 %custom-call.32 = f32[1,128,128]{1,2,0:T(8,128)S(1)} custom-call(f32[1,128,128]{2,1,0:T(8,128)S(1)} %get-tuple-element.60), custom_call_target="InvertDiagBlocksLowerTriangular" | custom-call | tf_op jit(solution)/shard_map/jit(cholesky)/cholesky | solution.py:10
  464.7 11.7 %cholesky.217 = f32[128,128]{1,0:T(8,128)S(1)} custom-call(f32[128,128]{1,0:T(8,128)S(1)} %cholesky.270), custom_call_target="Cholesky" | custom-call | tf_op jit(solution)/shard_map/jit(cholesky)/cholesky | solution.py:10
  476.4 10.2 %custom-call.33 = f32[1,128,128]{1,2,0:T(8,128)S(1)} custom-call(f32[1,128,128]{2,1,0:T(8,128)S(1)} %get-tuple-element.57), custom_call_target="InvertDiagBlocksLowerTriangular" | custom-call | tf_op jit(solution)/shard_map/jit(cholesky)/cholesky | solution.py:10
  487.3 11.7 %cholesky.238 = f32[128,128]{1,0:T(8,128)S(1)} custom-call(f32[128,128]{1,0:T(8,128)S(1)} %cholesky.275), custom_call_target="Cholesky" | custom-call | tf_op jit(solution)/shard_map/jit(cholesky)/cholesky | solution.py:10
  499.1 9.8 %custom-call.34 = f32[1,128,128]{1,2,0:T(8,128)S(1)} custom-call(f32[1,128,128]{2,1,0:T(8,128)S(1)} %get-tuple-element.54), custom_call_target="InvertDiagBlocksLowerTriangular" | custom-call | tf_op jit(solution)/shard_map/jit(cholesky)/cholesky | solution.py:10
  509.5 11.9 %cholesky.255 = f32[128,128]{1,0:T(8,128)S(1)} custom-call(f32[128,128]{1,0:T(8,128)S(1)} %convolution_subtract_fusion.6), custom_call_target="Cholesky" | custom-call | tf_op jit(solution)/shard_map/jit(cholesky)/cholesky | solution.py:10
  521.3 0.7 compare_reduce_fusion.27
  523.4 0.6 compare_reduce_fusion.26
  524.7 0.6 compare_reduce_fusion.25
  526.7 10.7 %while.1 = (s32[]{:T(128)}, f32[512,512]{1,0:T(8,128)S(1)}, s32[4,2]{0,1:T(2,128)S(1)}, f32[4,128,128]{2,1,0:T(8,128)}, s32[]{:T(128)}) while((s32[]{:T(128)}, f32[512,512]{1,0:T(8,128)S(1)}, s32[4,2]{0,1:T(2,128)S(1)}, f32[4,128,128]{2,1,0:T(8,128)}, s32[]{:T(128)}) %tuple.93), condition=%wide.while_cond, body=%wide.while_body.sunk | while | flops 2 | bytes 132705 | solution.py:12
  527.4 2.0 bitcast_dynamic-update-slice_fusion.2
  530.1 2.0 bitcast_dynamic-update-slice_fusion.2
  532.7 2.0 bitcast_dynamic-update-slice_fusion.2
  535.4 2.0 bitcast_dynamic-update-slice_fusion.2
  537.4 40.1 %custom-call.35 = f32[4,128,128]{1,2,0:T(8,128)S(1)} custom-call(f32[4,128,128]{2,1,0:T(8,128)} %get-tuple-element.13), custom_call_target="InvertDiagBlocksLowerTriangular" | custom-call | tf_op jit(solution)/shard_map/triangular_solve | solution.py:12
  578.2 1.5 fusion.39
  579.7 1.6 convolution_subtract_fusion.3
  581.3 0.6 fusion.64
  582.0 0.7 convolution_subtract_fusion.1
  583.4 1.1 fusion.19
  585.7 0.6 convolution_subtract_fusion.2
  586.9 0.7 convolution_subtract_fusion
  588.3 1.1 fusion.16
  590.0 2.6 add_convert_fusion
  592.6 70.8 %reduce-scatter.2.cloned.1.call-done = f32[32,1024]{1,0:T(8,128)} async-done(((f32[1024,1024]{1,0:T(8,128)}), f32[32,1024]{1,0:T(8,128)}) %reduce-scatter.2.cloned.1.call-update) | async-done | bytes 131088 | tf_op jit(solution)/shard_map/reduce_scatter | solution.py:56
  663.4 2.2 fusion.24
  (71 shorter events, 12.7 us)
Async XLA Ops:
  7.2 110.6 %all-gather.5.cloned.1.call-start = ((), (), s32[]{:S(2)}) async-start(), calls=%async_computation.2 | async-start | bytes 7569408 | tf_op jit(solution)/shard_map/all_gather | solution.py:48
  13.0 11.5 %copy-start.3 = (bf16[32,1024]{1,0:T(8,128)(2,1)S(1)}, bf16[32,1024]{1,0:T(8,128)(2,1)}, u32[]{:S(2)}) copy-start(bf16[32,1024]{1,0:T(8,128)(2,1)} %param.10) | copy-start | bytes 196612
  13.0 11.5 %copy-start.4 = (bf16[32,1024]{1,0:T(8,128)(2,1)S(1)}, bf16[32,1024]{1,0:T(8,128)(2,1)}, u32[]{:S(2)}) copy-start(bf16[32,1024]{1,0:T(8,128)(2,1)} %param.9) | copy-start | bytes 196612
  13.0 12.3 %copy-start.5 = (s32[32]{0:T(128)S(1)}, s32[32]{0:T(128)}, u32[]{:S(2)}) copy-start(s32[32]{0:T(128)} %param.6) | copy-start | bytes 388
  13.0 169.3 %all-to-all-start = ((bf16[32,32,896]{2,0,1:T(8,128)(2,1)}), bf16[32,32,896]{2,0,1:T(8,128)(2,1)S(1)}, u32[]{:S(2)}, u32[]{:S(2)}) async-start(bf16[32,32,896]{2,0,1:T(8,128)(2,1)} %bitcast.120), calls=%async_computation | async-start | bytes 3670016 | tf_op jit(solution)/shard_map/all_to_all | solution.py:47
  24.5 171.6 %all-gather.7.cloned.1.call-start = ((), (), s32[]{:S(2)}) async-start(), calls=%async_computation.3 | async-start | bytes 2162688 | tf_op jit(solution)/shard_map/all_gather | solution.py:60
  25.3 403.5 %all-gather.9.cloned.1.call-start = ((), (), s32[]{:S(2)}) async-start(), calls=%async_computation.5 | async-start | bytes 34603008 | tf_op jit(solution)/shard_map/all_gather | solution.py:53
  182.3 2.9 copy-start.1
  185.2 478.2 %reduce-scatter.2.cloned.1.call-start = ((), (), s32[]{:S(2)}) async-start(), calls=%async_computation.4 | async-start | bytes 4325376 | tf_op jit(solution)/shard_map/reduce_scatter | solution.py:56
  578.2 3.8 copy-start
  588.2 1.7 copy-start.2
  588.2 1.8 copy-start.6
  590.0 73.3 %copy-start.7 = (pred[32]{0:T(512)(128)(4,1)S(1)}, pred[32]{0:T(512)(128)(4,1)}, u32[]{:S(2)}) copy-start(pred[32]{0:T(512)(128)(4,1)} %compare_and_fusion) | copy-start | bytes 100
Sparse Core Ops, SparseCore 0:
  11.6 106.1 all-gather.4
  121.0 75.0 all-gather.6
  198.7 230.0 all-gather.8
  442.2 221.1 reduce-scatter.1
